TPU v7x, 256 devices: a whole 4x4x8 slice. The times are simulated.
256 devices in a mesh: tok: 32 (over x, z), head: 8 (over y, core).
Axes of the slice: x: 4, y: 4, z: 8, core: 2. Of those that a mesh axis runs over, the one named last changes fastest.
Arguments:
- tokens: bfloat16 [32768, 1664], P(('tok', 'head')), may hold values from -75 to 75
- attn_gain: float32 [1664], replicated, may hold values from 0.1 to 1.9
- qkv_weight: bfloat16 [3, 1664, 1664], P(None, 'head'), may hold values from -5 to 5
- out_weight: bfloat16 [1664, 1664], P('head'), may hold values from -0.4375 to 0.4375
- merge_gain: float32 [1664], replicated, may hold values from 0.1 to 1.9
- merge_weight: bfloat16 [6656, 4096], P('head', 'tok'), may hold values from -0.078125 to 0.078125
- grid_sizes: int32 [2, 128], P(None, 'tok'), may hold values from 2 to 16, as said below
- segment_ids: int32 [32768], P('tok'), may hold values from 0 to 127, as said below
- patch_pos: int32 [2, 32768], P(None, 'tok'), may hold values from 0 to 15, as said below
- live_mask: int32 [32768], P('tok'), may hold values from 0 to 1, as said below
- owners: int32 [8192, 1], P(('tok', 'head')), may hold values from 0 to 31; in each aligned block of 32 rows (0 to 31, 32 to 63, ...) at most 2 rows name the same one
Outputs:
- delivered: bfloat16 [16384, 4096], P(('tok', 'head'))
Inputs may be any that keep to these rules, and one draw needn't show every extreme that they name: `grid_sizes`: both sides of every image are even, and some image is 16 by 16. `segment_ids`: never fall along the tokens. The aligned block b of 1024 tokens holds images b * 4 to (b + 1) * 4 - 1 packed in order from the block's start, image s taking grid_sizes[0, s] * grid_sizes[1, s] tokens; the block's remaining tokens carry the number of its last image. `patch_pos`: an image's tokens come in 2x2 windows, windows in row-major order, each window as (2 * r, 2 * c), (2 * r, 2 * c + 1), (2 * r + 1, 2 * c), (2 * r + 1, 2 * c + 1); padding tokens sit at (0, 0). `live_mask`: 1 exactly on the tokens that belong to an image. `owners`: in each aligned block of 32 rows (the merged rows of one device) no owner is named more than 2 times.
All inputs are finite; a program needn't handle non-finite values.
Results may differ from a plain program's by a relative error of at most 0.024.
Values may be sent and summed in bfloat16 or wider, within the bound.
No kernel may reach another device: no remote copies, remote signals or barrier semaphores. Data moves between devices by JAX's collectives and lax.ppermute only.
A program may use at most 64 MiB of HBM per device.

v0:
```python
import jax
import jax.numpy as jnp
from jax import lax
from jax.sharding import PartitionSpec as P

D = 1664
HD = 104
SIDE = 16
EPSILON = 1e-06
NEGATIVE = -1e30


def layer_norm(values, gain_vec):
    average = jnp.mean(values, axis=-1, keepdims=True)
    centred = values - average
    variance = jnp.mean(centred * centred, axis=-1, keepdims=True)
    return centred * lax.rsqrt(variance + EPSILON) * gain_vec


def rotate(vectors, row_coord, col_coord):
    quarter = vectors.shape[-1] // 4
    frequency = 10000.0 ** (-jnp.arange(quarter, dtype=jnp.float32) / quarter)
    pieces = []
    for which_axis, coordinate in ((0, row_coord), (1, col_coord)):
        leading = vectors[..., 2 * which_axis * quarter : (2 * which_axis + 1) * quarter]
        trailing = vectors[..., (2 * which_axis + 1) * quarter : (2 * which_axis + 2) * quarter]
        angles = coordinate[:, None, None] * frequency
        cosine = jnp.cos(angles)
        sine_val = jnp.sin(angles)
        pieces.append(leading * cosine - trailing * sine_val)
        pieces.append(leading * sine_val + trailing * cosine)
    return jnp.concatenate(pieces, axis=-1)


def body(
    tokens,
    attn_gain,
    qkv_weight,
    out_weight,
    merge_gain,
    merge_weight,
    grid_sizes,
    segment_ids,
    patch_pos,
    live_mask,
    owners,
):
    group_len = segment_ids.shape[0]
    local_rows = tokens.shape[0]
    head_width = qkv_weight.shape[1]
    heads_here = head_width // HD
    tok_count = lax.axis_size("tok")
    image_count = grid_sizes.shape[1]
    local_image = segment_ids - lax.axis_index("tok") * image_count
    image_match = local_image[:, None] == jnp.arange(image_count, dtype=jnp.int32)[None, :]
    grid_float = grid_sizes.astype(jnp.float32)
    row_size = jnp.sum(jnp.where(image_match, grid_float[0][None, :], 0.0), axis=1)
    col_size = jnp.sum(jnp.where(image_match, grid_float[1][None, :], 0.0), axis=1)
    row_coord = patch_pos[0].astype(jnp.float32) * SIDE / row_size
    col_coord = patch_pos[1].astype(jnp.float32) * SIDE / col_size
    stacked_weight = qkv_weight.reshape(3 * head_width, D)
    normed = layer_norm(tokens.astype(jnp.float32), attn_gain).astype(jnp.bfloat16)
    projected_rows = lax.dot_general(
        lax.all_gather(normed, "head", axis=0, tiled=True),
        stacked_weight,
        (((1,), (1,)), ((), ())),
        preferred_element_type=jnp.float32,
    )
    projected_rows = projected_rows.reshape(group_len, 3, heads_here, HD)
    query_all = (rotate(projected_rows[:, 0], row_coord, col_coord) * HD ** (-0.5)).astype(
        jnp.bfloat16
    )
    key_all = rotate(projected_rows[:, 1], row_coord, col_coord).astype(jnp.bfloat16)
    value_all = projected_rows[:, 2].astype(jnp.bfloat16)
    block_len = min(512, group_len)
    block_count = group_len // block_len
    key_live = live_mask == 1

    def allowed_pairs(query_start, span):
        query_seg = lax.dynamic_slice_in_dim(segment_ids, query_start, block_len)
        query_place = query_start + jnp.arange(block_len, dtype=jnp.int32)
        key_place = jnp.arange(span, dtype=jnp.int32)
        same_image = query_seg[:, None] == segment_ids[None, :]
        return same_image & (key_live[None, :] | (query_place[:, None] == key_place[None, :]))

    def query_block(query_start):
        queries = lax.dynamic_slice_in_dim(query_all, query_start, block_len, 0)
        allowed = allowed_pairs(query_start, group_len)
        scores = jnp.einsum("qhd,khd->hqk", queries, key_all, preferred_element_type=jnp.float32)
        masked = jnp.where(allowed[None], scores, NEGATIVE)
        row_top = jnp.max(masked, axis=2, keepdims=True)
        exponent = jnp.where(allowed[None], jnp.exp(masked - row_top), 0.0)
        denominator = jnp.sum(exponent, axis=2)
        numerator = jnp.einsum(
            "hqk,khd->qhd",
            exponent.astype(jnp.bfloat16),
            value_all,
            preferred_element_type=jnp.float32,
        )
        return (numerator / denominator.T[:, :, None]).astype(jnp.bfloat16)

    block_starts = jnp.arange(block_count, dtype=jnp.int32) * block_len
    heads_out = lax.map(query_block, block_starts).reshape(group_len, head_width)
    attn_rows = lax.psum_scatter(
        jnp.dot(heads_out, out_weight, preferred_element_type=jnp.float32).astype(jnp.bfloat16),
        "head",
        scatter_dimension=0,
        tiled=True,
    ).astype(jnp.float32)
    stream = (tokens.astype(jnp.float32) + attn_rows).reshape(local_rows // 4, 4, D)
    average = jnp.sum(stream, axis=2, keepdims=True) / D
    variance = jnp.sum(stream * stream, axis=2, keepdims=True) / D - average * average
    window_rows = ((stream - average) * lax.rsqrt(variance + EPSILON) * merge_gain).astype(
        jnp.bfloat16
    )
    merged_slice = lax.all_to_all(
        window_rows.reshape(local_rows // 4, 4 * D), "head", split_axis=1, concat_axis=0, tiled=True
    )
    merged_count = local_rows // 4
    column_terms = jnp.dot(
        merged_slice,
        lax.all_gather(merge_weight, "tok", axis=1, tiled=True),
        preferred_element_type=jnp.float32,
    )
    projected = lax.psum_scatter(
        column_terms.astype(jnp.bfloat16), "head", scatter_dimension=0, tiled=True
    )
    slot_count = max(2, 2 * merged_count // tok_count)
    owner_col = owners[:, 0]
    owner_hot = (owner_col[:, None] == jnp.arange(tok_count, dtype=jnp.int32)[None, :]).astype(
        jnp.int32
    )
    earlier = jnp.cumsum(owner_hot, axis=0, dtype=jnp.int32) - owner_hot
    slot_index = jnp.sum(earlier * owner_hot, axis=1, dtype=jnp.int32)
    target = owner_col * slot_count + slot_index
    select = (
        jnp.arange(tok_count * slot_count, dtype=jnp.int32)[:, None] == target[None, :]
    ).astype(jnp.bfloat16)
    send_rows = jnp.dot(select, projected, preferred_element_type=jnp.float32).astype(jnp.bfloat16)
    send_rows = send_rows.reshape(tok_count, slot_count, -1)
    received = lax.all_to_all(send_rows, "tok", split_axis=0, concat_axis=0, tiled=True)
    return received.reshape(tok_count * slot_count, -1)


def solution(mesh):
    placed = (
        P(("tok", "head"), None),
        P(),
        P(None, "head", None),
        P("head", None),
        P(),
        P("head", "tok"),
        P(None, "tok"),
        P("tok"),
        P(None, "tok"),
        P("tok"),
        P(("tok", "head"), None),
    )
    return jax.shard_map(
        body, mesh=mesh, in_specs=placed, out_specs=P(("tok", "head"), None), check_vma=False
    )
```

profile of v0, /device:TPU:57, one launch (start us, length us, event | category | flops | bytes accessed | tf_op | source)
XLA Modules:
  0.0 257.5 jit_solution(5983882378429077472)
XLA Ops:
  7.4 1.3 convert_reduce_fusion
  8.7 1.3 fusion.46
  10.0 2.1 fusion.48
  12.1 0.7 convert_element_type.65
  12.8 0.7 broadcast_subtract_fusion
  13.5 0.1 select_reduce_fusion.2
  13.6 0.8 convert_multiply_fusion.1
  14.4 0.7 broadcast_compare_fusion
  15.1 1.0 multiply_cosine_fusion.1
  16.1 28.8 %all-gather.3.cloned.1.call-done = bf16[1024,1664]{1,0:T(8,128)(2,1)} async-done(((bf16[128,1664]{1,0:T(8,128)(2,1)}), bf16[1024,1664]{1,0:T(8,128)(2,1)}) %all-gather.3.cloned.1.call-update) | async-done | bytes 3407888 | tf_op jit(solution)/shard_map/all_gather | solution.py:64
  44.9 4.5 %fusion.39 = f32[1024,3,2,104]{0,3,2,1:T(8,128)S(1)} fusion(bf16[3,2,104,1664]{3,2,1,0:T(8,128)(2,1)S(1)} %bitcast.70, bf16[1024,1664]{1,0:T(8,128)(2,1)} %all-gather.3.cloned.1.call-done), kind=kOutput, calls=%fused_computation.27 | convolution fusion | flops 2126512128 | bytes 8040448 | tf_op jit(solution)/shard_map/dot_general | solution.py:63
  49.4 0.2 slice_bitcast_fusion
  49.6 0.8 fusion.50
  50.4 0.2 subtract_convert_fusion.1
  50.6 0.2 multiply_subtract_fusion.1
  50.8 0.9 pad_maximum_fusion
  51.7 0.9 fusion.49
  52.6 23.1 %while.10 = (s32[]{:T(128)}, bf16[2,512,2,104]{1,3,2,0:T(8,128)(2,1)}, s32[2]{0:T(128)S(1)}, s32[1024]{0:T(1024)S(1)}, pred[1024]{0:T(1024)(128)(4,1)S(1)}, /*in...) while((s32[]{:T(128)}, ...), condition=%wide.region_9.10_spmd, body=%wide.region_6.0_spmd.sunk | while | flops 443762176 | bytes 7069351 | solution.py:103
  52.6 0.6 dynamic_slice.26
  55.1 0.1 dynamic_slice.27
  55.1 0.6 iota_add_fusion.2
  55.8 0.7 fusion.80
  56.4 4.6 %fusion.81 = (f32[2,512]{1,0:T(2,128)S(1)}, bf16[2,512,1024]{2,1,0:T(8,128)(2,1)}) fusion(pred[512,1024]{1,0:T(8,128)(4,1)S(1)} %fusion.80, bf16[1024,2,104]{0,2,1:T(8,128)(2,1)} %get-tuple-element.180, bf16[1024,2,104]{0,2,1:T(8,128)(2,1)} %get-tuple-element.179, s32[]{:T(128)S(6)} %select_n.34), kind=kOutput, calls=%fused_computation.84.clone.1 | convolution fusion | flops 223347712 | bytes 3788804 | tf_op jit(solution)/shard_map/while/body/eval_jaxpr/sub | solution.py:92
  61.0 3.1 %fusion.82 = bf16[2,512,2,104]{1,3,2,0:T(8,128)(2,1)} fusion(bf16[2,512,2,104]{1,3,2,0:T(8,128)(2,1)} %get-tuple-element.164, s32[]{:T(128)} %get-tuple-element.163, bf16[1024,2,104]{0,2,1:T(8,128)(2,1)} %get-tuple-element.181, bf16[2,512,1024]{2,1,0:T(8,128)(2,1)} %get-tuple-element.150, f32[512,2]{0,1:T(2,128)S(1)} %bitcast.80), kind=kOutput, calls=%fused_computation.15.clone.1 | convolution fusion | flops 218316800 | bytes 2740736 | tf_op jit(solution)/shard_map/while/body/eval_jaxpr/hqk,khd->qhd/dot_general | solution.py:94
  64.1 0.6 dynamic_slice.26
  66.7 0.6 iota_add_fusion.2
  67.3 0.7 fusion.80
  68.0 4.6 %fusion.81 = (f32[2,512]{1,0:T(2,128)S(1)}, bf16[2,512,1024]{2,1,0:T(8,128)(2,1)}) fusion(pred[512,1024]{1,0:T(8,128)(4,1)S(1)} %fusion.80, bf16[1024,2,104]{0,2,1:T(8,128)(2,1)} %get-tuple-element.180, bf16[1024,2,104]{0,2,1:T(8,128)(2,1)} %get-tuple-element.179, s32[]{:T(128)S(6)} %select_n.34), kind=kOutput, calls=%fused_computation.84.clone.1 | convolution fusion | flops 223347712 | bytes 3788804 | tf_op jit(solution)/shard_map/while/body/eval_jaxpr/sub | solution.py:92
  72.6 3.1 %fusion.82 = bf16[2,512,2,104]{1,3,2,0:T(8,128)(2,1)} fusion(bf16[2,512,2,104]{1,3,2,0:T(8,128)(2,1)} %get-tuple-element.164, s32[]{:T(128)} %get-tuple-element.163, bf16[1024,2,104]{0,2,1:T(8,128)(2,1)} %get-tuple-element.181, bf16[2,512,1024]{2,1,0:T(8,128)(2,1)} %get-tuple-element.150, f32[512,2]{0,1:T(2,128)S(1)} %bitcast.80), kind=kOutput, calls=%fused_computation.15.clone.1 | convolution fusion | flops 218316800 | bytes 2740736 | tf_op jit(solution)/shard_map/while/body/eval_jaxpr/hqk,khd->qhd/dot_general | solution.py:94
  75.7 1.4 copy.16
  77.2 3.0 %convolution_convert_fusion.2 = bf16[1024,1664]{1,0:T(8,128)(2,1)} fusion(bf16[1024,208]{0,1:T(8,128)(2,1)S(1)} %bitcast.71, bf16[208,1664]{1,0:T(8,128)(2,1)S(1)} %copy-done.2), kind=kOutput, calls=%fused_computation.26 | convolution fusion | flops 710541312 | bytes 4526080 | tf_op jit(solution)/shard_map/dot_general | solution.py:105
  80.3 0.5 all-gather.5.cloned.1.call-update
  80.9 0.1 mul.313
  81.0 38.2 %reduce-scatter.3.cloned.1.call-done = bf16[128,1664]{1,0:T(8,128)(2,1)} async-done(((bf16[1024,1664]{1,0:T(8,128)(2,1)}), bf16[128,1664]{1,0:T(8,128)(2,1)}) %reduce-scatter.3.cloned.1.call-update) | async-done | bytes 426000 | tf_op jit(solution)/shard_map/reduce_scatter | solution.py:104
  119.2 2.1 fusion.53
  121.3 0.1 div.50
  121.4 0.1 div.52
  121.7 1.4 reshape.306
  123.1 0.3 fusion.45
  123.4 11.3 %all_to_all.21 = bf16[32,8,832]{2,0,1:T(8,128)(2,1)S(1)} all-to-all(bf16[32,8,832]{2,0,1:T(8,128)(2,1)S(1)} %fusion.45), channel_id=1, replica_groups=mesh['tok'=32,'head'=8] {'head'}, dimensions={1} | all-to-all | bytes 851968 | tf_op jit(solution)/shard_map/all_to_all | solution.py:116
  134.7 39.1 %all-gather.5.cloned.1.call-done = bf16[832,4096]{1,0:T(8,128)(2,1)} async-done(((bf16[832,128]{1,0:T(8,128)(2,1)}), bf16[832,4096]{1,0:T(8,128)(2,1)}) %all-gather.5.cloned.1.call-update) | async-done | bytes 6815760 | tf_op jit(solution)/shard_map/all_gather | solution.py:122
  173.8 6.8 %convolution_convert_fusion = bf16[256,4096]{1,0:T(8,128)(2,1)} fusion(bf16[256,832]{1,0:T(8,128)(2,1)S(1)} %bitcast.73, bf16[832,4096]{1,0:T(8,128)(2,1)} %all-gather.5.cloned.1.call-done), kind=kOutput, calls=%fused_computation.24 | convolution fusion | flops 1745879040 | bytes 9338880 | tf_op jit(solution)/shard_map/dot_general | solution.py:120
  180.7 0.2 select_reduce_fusion.3
  180.9 39.6 %reduce-scatter.5.cloned.1.call-done = bf16[32,4096]{1,0:T(8,128)(2,1)} async-done(((bf16[256,4096]{1,0:T(8,128)(2,1)}), bf16[32,4096]{1,0:T(8,128)(2,1)}) %reduce-scatter.5.cloned.1.call-update) | async-done | bytes 262160 | tf_op jit(solution)/shard_map/reduce_scatter | solution.py:125
  220.5 1.2 convolution_convert_fusion.1
  221.7 0.3 reshape.307
  222.1 27.3 %all_to_all.22 = bf16[32,2,4096]{2,1,0:T(2,128)(2,1)S(1)} all-to-all(bf16[32,2,4096]{2,1,0:T(2,128)(2,1)S(1)} %reshape.307), channel_id=1, replica_groups=mesh['tok'=32,'head'=8] {'tok'}, dimensions={0} | all-to-all | bytes 1048576 | tf_op jit(solution)/shard_map/all_to_all | solution.py:141
  249.4 1.0 reshape.308
  (40 shorter events, 0.8 us)
Async XLA Ops:
  7.4 37.5 %copy-start = (bf16[3,208,1664]{2,1,0:T(8,128)(2,1)S(1)}, bf16[3,208,1664]{2,1,0:T(8,128)(2,1)}, u32[]{:S(2)}) copy-start(bf16[3,208,1664]{2,1,0:T(8,128)(2,1)} %param.15) | copy-start | bytes 6230020
  7.4 37.5 %all-gather.3.cloned.1.call-start = ((), (), s32[]{:S(2)}) async-start(), calls=%async_computation.4 | async-start | bytes 3833856 | tf_op jit(solution)/shard_map/all_gather | solution.py:64
  12.1 107.1 %reduce-scatter.3.cloned.1.call-start = ((), (), s32[]{:S(2)}) async-start(), calls=%async_computation.5 | async-start | bytes 3833856 | tf_op jit(solution)/shard_map/reduce_scatter | solution.py:104
  50.4 2.2 copy-start.3
  52.6 24.6 %copy-start.2 = (bf16[208,1664]{1,0:T(8,128)(2,1)S(1)}, bf16[208,1664]{1,0:T(8,128)(2,1)}, u32[]{:S(2)}) copy-start(bf16[208,1664]{1,0:T(8,128)(2,1)} %param.16) | copy-start | bytes 2076676
  80.2 0.7 copy-start.4
  80.2 39.0 %copy-start.1 = (bf16[128,1664]{1,0:T(8,128)(2,1)S(1)}, bf16[128,1664]{1,0:T(8,128)(2,1)}, u32[]{:S(2)}) copy-start(bf16[128,1664]{1,0:T(8,128)(2,1)} %param.13) | copy-start | bytes 1277956
  80.2 93.6 %all-gather.5.cloned.1.call-start = ((), (), s32[]{:S(2)}) async-start(), calls=%async_computation.6 | async-start | bytes 7028736 | tf_op jit(solution)/shard_map/all_gather | solution.py:122
  80.8 139.7 %reduce-scatter.5.cloned.1.call-start = ((), (), s32[]{:S(2)}) async-start(), calls=%async_computation.7 | async-start | bytes 2359296 | tf_op jit(solution)/shard_map/reduce_scatter | solution.py:125
  173.8 6.8 %copy-start.5 = (s32[32,1]{0,1:T(1,128)S(1)}, s32[32,1]{0,1:T(1,128)}, u32[]{:S(2)}) copy-start(s32[32,1]{0,1:T(1,128)} %param.23) | copy-start | bytes 388
Sparse Core Ops, SparseCore 0:
  12.2 32.6 all-gather.2
  80.3 38.8 reduce-scatter.2
  180.7 39.7 reduce-scatter.4
Sparse Core Ops, SparseCore 1:
  83.2 90.5 all-gather.4
where the time goes:
time: 258 us; the launch traced here: 257 us
  waiting for transfers between devices  146 us (57%)
  blocking collectives  38.6 us (15%)
  matrix products  30.8 us (12%)
  other arithmetic  16.1 us (6%)
  between operations  14.7 us (6%)
  local copies, waits for them, and re-layouts  7.14 us (3%)
  loops' own time  3.76 us (1%)
    reduce_scatter x1, waiting for transfers between devices, body(): lax.psum_scatter(column_terms.astype(jnp.bfloat16), 'head', scatter_dimen...  39.6 us
    all_gather x1, waiting for transfers between devices, body(): lax.all_gather(merge_weight, 'tok', axis=1, tiled=True)  39.1 us
    reduce_scatter x1, waiting for transfers between devices, body(): lax.psum_scatter(jnp.dot(heads_out, out_weight, preferred_element_type=jn...  38.2 us
    all_gather x1, waiting for transfers between devices, body(): lax.all_gather(normed, 'head', axis=0, tiled=True)  28.8 us
    all_to_all x1, blocking collectives, body(): lax.all_to_all(send_rows, 'tok', split_axis=0, concat_axis=0, tiled=True)  27.3 us
    all_to_all x1, blocking collectives, body(): lax.all_to_all(window_rows.reshape(local_rows // 4, 4 * D), 'head', split...  11.3 us
    sub x2, matrix products, query_block(): exponent = jnp.where(allowed[None], jnp.exp(masked - row_top), 0.0)  9.22 us
    dot_general x1, matrix products, body(): jnp.dot(merged_slice, lax.all_gather(merge_weight, 'tok', axis=1, tiled=T...  6.76 us
  transfers between devices with their start and end apart: 4, of which 4 were waited for; matrix products, arithmetic and copies ran while one was open for 3% of the time, Pallas kernels for 0%

commit v1 on v0

--- a/solution.py
+++ b/solution.py
@@ -61,7 +61,9 @@
     stacked_weight = qkv_weight.reshape(3 * head_width, D)
     normed = layer_norm(tokens.astype(jnp.float32), attn_gain).astype(jnp.bfloat16)
     projected_rows = lax.dot_general(
-        lax.all_gather(normed, "head", axis=0, tiled=True),
+        jnp.concatenate(
+            lax.all_to_all(jnp.stack([normed] * lax.axis_size("head")), "head", 0, 0), axis=0
+        ),
         stacked_weight,
         (((1,), (1,)), ((), ())),
         preferred_element_type=jnp.float32,

time: 258 us -> 273 us (1.058)
  waiting for transfers between devices: 146 us -> 156 us
  starting transfers between devices: 0.13 us -> 5.2 us
  other arithmetic: 16.1 us -> 12.6 us
    all_to_all x0 -> x1, waiting for transfers between devices: none -> 37.4 us  [body(): lax.all_to_all(jnp.stack([normed] * lax.axis_size('head')), 'head', 0, 0)]
    all_gather x1 -> x0, waiting for transfers between devices: 28.8 us -> none  [body(): lax.all_gather(normed, 'head', axis=0, tiled=True)]
    all_to_all x0 -> x1, starting transfers between devices: none -> 5.12 us  [body(): lax.all_to_all(jnp.stack([normed] * lax.axis_size('head')), 'head', 0, 0)]
  transfers between devices with their start and end apart: 4 -> 4, of which waited for: 4 -> 4; matrix products, arithmetic and copies ran while one was open for 3% -> 2% of each run, Pallas kernels for 0% -> 0%
where the time goes in v1:
time: 273 us; the launch traced here: 272 us
  waiting for transfers between devices  156 us (57%)
  blocking collectives  38.5 us (14%)
  matrix products  30.9 us (11%)
  between operations  15.1 us (6%)
  other arithmetic  12.6 us (5%)
  local copies, waits for them, and re-layouts  9.29 us (3%)
  starting transfers between devices  5.2 us (2%)
  loops' own time  4.18 us (2%)
    reduce_scatter x1, waiting for transfers between devices, body(): lax.psum_scatter(jnp.dot(heads_out, out_weight, preferred_element_type=jn...  39.7 us
    reduce_scatter x1, waiting for transfers between devices, body(): lax.psum_scatter(column_terms.astype(jnp.bfloat16), 'head', scatter_dimen...  39.6 us
    all_gather x1, waiting for transfers between devices, body(): lax.all_gather(merge_weight, 'tok', axis=1, tiled=True)  39.1 us
    all_to_all x1, waiting for transfers between devices, body(): lax.all_to_all(jnp.stack([normed] * lax.axis_size('head')), 'head', 0, 0)  37.4 us
    all_to_all x1, blocking collectives, body(): lax.all_to_all(send_rows, 'tok', split_axis=0, concat_axis=0, tiled=True)  27.2 us
    all_to_all x1, blocking collectives, body(): lax.all_to_all(window_rows.reshape(local_rows // 4, 4 * D), 'head', split...  11.2 us
    sub x2, matrix products, query_block(): exponent = jnp.where(allowed[None], jnp.exp(masked - row_top), 0.0)  9.23 us
    dot_general x1, matrix products, body(): jnp.dot(merged_slice, lax.all_gather(merge_weight, 'tok', axis=1, tiled=T...  6.76 us
  transfers between devices with their start and end apart: 4, of which 4 were waited for; matrix products, arithmetic and copies ran while one was open for 2% of the time, Pallas kernels for 0%

profile of v1, /device:TPU:57, one launch (start us, length us, event | category | flops | bytes accessed | tf_op | source)
XLA Modules:
  0.0 272.1 jit_solution(9222613179299946320)
XLA Ops:
  7.4 1.3 convert_reduce_fusion
  8.7 1.3 fusion.44
  9.9 1.3 fusion.46
  11.3 2.0 stack.2
  13.3 5.1 %all-to-all-start = ((bf16[8,128,1664]{2,1,0:T(8,128)(2,1)}), bf16[8,128,1664]{2,1,0:T(8,128)(2,1)}, u32[]{:S(2)}, u32[]{:S(2)}) async-start(bf16[8,128,1664]{2,1,0:T(8,128)(2,1)} %stack.2), calls=%async_computation | async-start | bytes 6815744 | tf_op jit(solution)/shard_map/all_to_all | solution.py:65
  18.5 0.1 select_reduce_fusion.2
  18.7 1.0 multiply_cosine_fusion.1
  19.7 37.4 %all-to-all-done = bf16[8,128,1664]{2,1,0:T(8,128)(2,1)} async-done(((bf16[8,128,1664]{2,1,0:T(8,128)(2,1)}), bf16[8,128,1664]{2,1,0:T(8,128)(2,1)}, u32[]{:S(2)}, u32[]{:S(2)}) %all-to-all-start) | async-done | bytes 3407904 | tf_op jit(solution)/shard_map/all_to_all | solution.py:65
  57.1 4.5 %fusion.57 = f32[1024,3,2,104]{0,3,2,1:T(8,128)S(1)} fusion(bf16[1024,1664,1,1]{1,0,3,2:T(8,128)(2,1)} %bitcast.7, bf16[3,2,104,1664]{3,2,1,0:T(8,128)(2,1)S(1)} %bitcast.71), kind=kOutput, calls=%fused_computation.83 | convolution fusion | flops 2126512128 | bytes 8040448 | tf_op jit(solution)/shard_map/dot_general | solution.py:63
  61.6 0.2 slice_bitcast_fusion
  61.8 0.8 fusion.48
  62.6 0.2 subtract_convert_fusion.1
  62.8 0.2 multiply_subtract_fusion.1
  63.0 0.9 pad_maximum_fusion
  63.9 0.9 fusion.47
  64.8 23.8 %while.10 = (s32[]{:T(128)}, bf16[2,512,2,104]{1,3,2,0:T(8,128)(2,1)}, s32[2]{0:T(128)S(1)}, s32[1024]{0:T(1024)S(1)}, pred[1024]{0:T(1024)(128)(4,1)S(1)}, /*in...) while((s32[]{:T(128)}, ...), condition=%wide.region_9.10_spmd, body=%wide.region_6.0_spmd.sunk | while | flops 443762176 | bytes 7069351 | solution.py:105
  64.8 0.7 dynamic_slice.26
  67.5 0.1 dynamic_slice.27
  67.6 0.7 iota_add_fusion.2
  68.3 0.7 fusion.80
  69.0 4.6 %fusion.81 = (f32[2,512]{1,0:T(2,128)S(1)}, bf16[2,512,1024]{2,1,0:T(8,128)(2,1)}) fusion(pred[512,1024]{1,0:T(8,128)(4,1)S(1)} %fusion.80, bf16[1024,2,104]{0,2,1:T(8,128)(2,1)} %get-tuple-element.180, bf16[1024,2,104]{0,2,1:T(8,128)(2,1)} %get-tuple-element.179, s32[]{:T(128)S(6)} %select_n.34), kind=kOutput, calls=%fused_computation.82.clone.1 | convolution fusion | flops 223347712 | bytes 3788804 | tf_op jit(solution)/shard_map/while/body/eval_jaxpr/sub | solution.py:94
  73.6 3.1 %fusion.82 = bf16[2,512,2,104]{1,3,2,0:T(8,128)(2,1)} fusion(bf16[2,512,2,104]{1,3,2,0:T(8,128)(2,1)} %get-tuple-element.164, s32[]{:T(128)} %get-tuple-element.163, bf16[1024,2,104]{0,2,1:T(8,128)(2,1)} %get-tuple-element.181, bf16[2,512,1024]{2,1,0:T(8,128)(2,1)} %get-tuple-element.150, f32[512,2]{0,1:T(2,128)S(1)} %bitcast.81), kind=kOutput, calls=%fused_computation.15.clone.1 | convolution fusion | flops 218316800 | bytes 2740736 | tf_op jit(solution)/shard_map/while/body/eval_jaxpr/hqk,khd->qhd/dot_general | solution.py:96
  76.7 0.7 dynamic_slice.26
  79.4 0.1 dynamic_slice.27
  79.5 0.7 iota_add_fusion.2
  80.2 0.7 fusion.80
  80.9 4.6 %fusion.81 = (f32[2,512]{1,0:T(2,128)S(1)}, bf16[2,512,1024]{2,1,0:T(8,128)(2,1)}) fusion(pred[512,1024]{1,0:T(8,128)(4,1)S(1)} %fusion.80, bf16[1024,2,104]{0,2,1:T(8,128)(2,1)} %get-tuple-element.180, bf16[1024,2,104]{0,2,1:T(8,128)(2,1)} %get-tuple-element.179, s32[]{:T(128)S(6)} %select_n.34), kind=kOutput, calls=%fused_computation.82.clone.1 | convolution fusion | flops 223347712 | bytes 3788804 | tf_op jit(solution)/shard_map/while/body/eval_jaxpr/sub | solution.py:94
  85.5 3.1 %fusion.82 = bf16[2,512,2,104]{1,3,2,0:T(8,128)(2,1)} fusion(bf16[2,512,2,104]{1,3,2,0:T(8,128)(2,1)} %get-tuple-element.164, s32[]{:T(128)} %get-tuple-element.163, bf16[1024,2,104]{0,2,1:T(8,128)(2,1)} %get-tuple-element.181, bf16[2,512,1024]{2,1,0:T(8,128)(2,1)} %get-tuple-element.150, f32[512,2]{0,1:T(2,128)S(1)} %bitcast.81), kind=kOutput, calls=%fused_computation.15.clone.1 | convolution fusion | flops 218316800 | bytes 2740736 | tf_op jit(solution)/shard_map/while/body/eval_jaxpr/hqk,khd->qhd/dot_general | solution.py:96
  88.6 1.4 copy.16
  90.1 3.0 %convolution_convert_fusion.2 = bf16[1024,1664]{1,0:T(8,128)(2,1)} fusion(bf16[1024,208]{0,1:T(8,128)(2,1)S(1)} %bitcast.72, bf16[208,1664]{1,0:T(8,128)(2,1)S(1)} %copy-done.2), kind=kOutput, calls=%fused_computation.26 | convolution fusion | flops 710541312 | bytes 4526080 | tf_op jit(solution)/shard_map/dot_general | solution.py:107
  93.1 0.5 all-gather.2.cloned.1.call-update
  93.8 0.1 mul.313
  93.9 39.7 %reduce-scatter.3.cloned.1.call-done = bf16[128,1664]{1,0:T(8,128)(2,1)} async-done(((bf16[1024,1664]{1,0:T(8,128)(2,1)}), bf16[128,1664]{1,0:T(8,128)(2,1)}) %reduce-scatter.3.cloned.1.call-update) | async-done | bytes 426000 | tf_op jit(solution)/shard_map/reduce_scatter | solution.py:106
  133.6 2.1 fusion.51
  135.7 0.1 div.50
  135.8 0.1 div.52
  135.9 0.1 copy.17
  136.1 1.4 reshape.312
  137.5 0.3 fusion.43
  137.9 11.2 %all_to_all.26 = bf16[32,8,832]{2,0,1:T(8,128)(2,1)S(1)} all-to-all(bf16[32,8,832]{2,0,1:T(8,128)(2,1)S(1)} %fusion.43), channel_id=1, replica_groups=mesh['tok'=32,'head'=8] {'head'}, dimensions={1} | all-to-all | bytes 851968 | tf_op jit(solution)/shard_map/all_to_all | solution.py:118
  149.1 39.1 %all-gather.2.cloned.1.call-done = bf16[832,4096]{1,0:T(8,128)(2,1)} async-done(((bf16[832,128]{1,0:T(8,128)(2,1)}), bf16[832,4096]{1,0:T(8,128)(2,1)}) %all-gather.2.cloned.1.call-update) | async-done | bytes 6815760 | tf_op jit(solution)/shard_map/all_gather | solution.py:124
  188.2 6.8 %convolution_convert_fusion = bf16[256,4096]{1,0:T(8,128)(2,1)} fusion(bf16[256,832]{1,0:T(8,128)(2,1)S(1)} %bitcast.74, bf16[832,4096]{1,0:T(8,128)(2,1)} %all-gather.2.cloned.1.call-done), kind=kOutput, calls=%fused_computation.24 | convolution fusion | flops 1745879040 | bytes 9338880 | tf_op jit(solution)/shard_map/dot_general | solution.py:122
  195.1 0.2 select_reduce_fusion.3
  195.3 39.6 %reduce-scatter.5.cloned.1.call-done = bf16[32,4096]{1,0:T(8,128)(2,1)} async-done(((bf16[256,4096]{1,0:T(8,128)(2,1)}), bf16[32,4096]{1,0:T(8,128)(2,1)}) %reduce-scatter.5.cloned.1.call-update) | async-done | bytes 262160 | tf_op jit(solution)/shard_map/reduce_scatter | solution.py:127
  234.9 1.2 convolution_convert_fusion.1
  236.1 0.3 reshape.313
  236.5 27.2 %all_to_all.27 = bf16[32,2,4096]{2,1,0:T(2,128)(2,1)S(1)} all-to-all(bf16[32,2,4096]{2,1,0:T(2,128)(2,1)S(1)} %reshape.313), channel_id=1, replica_groups=mesh['tok'=32,'head'=8] {'tok'}, dimensions={0} | all-to-all | bytes 1048576 | tf_op jit(solution)/shard_map/all_to_all | solution.py:143
  263.7 1.0 reshape.314
  (46 shorter events, 0.6 us)
Async XLA Ops:
  7.4 49.7 %copy-start = (bf16[3,208,1664]{2,1,0:T(8,128)(2,1)S(1)}, bf16[3,208,1664]{2,1,0:T(8,128)(2,1)}, u32[]{:S(2)}) copy-start(bf16[3,208,1664]{2,1,0:T(8,128)(2,1)} %param.15) | copy-start | bytes 6230020
  13.3 5.1 %copy-start.8 = (s32[2,4]{1,0:T(2,128)S(1)}, s32[2,4]{1,0:T(2,128)}, u32[]{:S(2)}) copy-start(s32[2,4]{1,0:T(2,128)} %param.19) | copy-start | bytes 100
  13.3 5.2 %copy-start.3 = (s32[1024]{0:T(1024)S(1)}, s32[1024]{0:T(1024)}, u32[]{:S(2)}) copy-start(s32[1024]{0:T(1024)} %param.20) | copy-start | bytes 12292
  13.3 5.3 %copy-start.4 = (s32[2,1024]{1,0:T(2,128)S(1)}, s32[2,1024]{1,0:T(2,128)}, u32[]{:S(2)}) copy-start(s32[2,1024]{1,0:T(2,128)} %param.21) | copy-start | bytes 24580
  13.3 5.4 %copy-start.6 = (s32[1024]{0:T(1024)S(1)}, s32[1024]{0:T(1024)}, u32[]{:S(2)}) copy-start(s32[1024]{0:T(1024)} %param.22) | copy-start | bytes 12292
  13.3 43.8 %all-to-all-start = ((bf16[8,128,1664]{2,1,0:T(8,128)(2,1)}), bf16[8,128,1664]{2,1,0:T(8,128)(2,1)}, u32[]{:S(2)}, u32[]{:S(2)}) async-start(bf16[8,128,1664]{2,1,0:T(8,128)(2,1)} %stack.2), calls=%async_computation | async-start | bytes 6815744 | tf_op jit(solution)/shard_map/all_to_all | solution.py:65
  18.4 115.2 %reduce-scatter.3.cloned.1.call-start = ((), (), s32[]{:S(2)}) async-start(), calls=%async_computation.5 | async-start | bytes 3833856 | tf_op jit(solution)/shard_map/reduce_scatter | solution.py:106
  64.8 25.3 %copy-start.2 = (bf16[208,1664]{1,0:T(8,128)(2,1)S(1)}, bf16[208,1664]{1,0:T(8,128)(2,1)}, u32[]{:S(2)}) copy-start(bf16[208,1664]{1,0:T(8,128)(2,1)} %param.16) | copy-start | bytes 2076676
  93.1 0.7 copy-start.5
  93.1 40.5 %copy-start.1 = (bf16[128,1664]{1,0:T(8,128)(2,1)S(1)}, bf16[128,1664]{1,0:T(8,128)(2,1)}, u32[]{:S(2)}) copy-start(bf16[128,1664]{1,0:T(8,128)(2,1)} %param.13) | copy-start | bytes 1277956
  93.1 95.1 %all-gather.2.cloned.1.call-start = ((), (), s32[]{:S(2)}) async-start(), calls=%async_computation.6 | async-start | bytes 7028736 | tf_op jit(solution)/shard_map/all_gather | solution.py:124
  93.7 141.2 %reduce-scatter.5.cloned.1.call-start = ((), (), s32[]{:S(2)}) async-start(), calls=%async_computation.7 | async-start | bytes 2359296 | tf_op jit(solution)/shard_map/reduce_scatter | solution.py:127
  188.2 6.8 %copy-start.7 = (s32[32,1]{0,1:T(1,128)S(1)}, s32[32,1]{0,1:T(1,128)}, u32[]{:S(2)}) copy-start(s32[32,1]{0,1:T(1,128)} %param.23) | copy-start | bytes 388
Sparse Core Ops, SparseCore 0:
  93.2 40.3 reduce-scatter.2
  195.1 39.7 reduce-scatter.4
Sparse Core Ops, SparseCore 1:
  96.0 92.1 all-gather.1
